TPU v7x, 128 devices: a whole 4x4x4 slice. The times are simulated.
128 devices in a mesh: section: 2 (over core), seq: 64 (over z, x, y).
Axes of the slice: x: 4, y: 4, z: 4, core: 2. Of those that a mesh axis runs over, the one named last changes fastest.
Arguments:
- patches: bfloat16 [32768, 1408], P('seq'), may hold values from -42 to 42
- image_grid: int32 [256, 2], P('seq'), may hold values from 2 to 52, as said below
- image_offsets: int32 [256], P('seq'), may hold values from 0 to 32736, as said below
- dest_positions: int32 [8192], replicated, may hold values from 0 to 16383, as said below
- text_embeds: bfloat16 [256, 64, 1408], P(None, 'seq'), may hold values from -42 to 42
- segment_ids: int32 [256, 64], replicated, may hold values from 0 to 3, as said below
- vision_qkv: bfloat16 [1408, 3, 1408], P(None, None, 'section'), may hold values from -0.15625 to 0.15625
- vision_out: bfloat16 [1408, 1408], P('section'), may hold values from -0.875 to 0.875
- projector: bfloat16 [4, 1408, 1408], P('section'), may hold values from -0.078125 to 0.078125
- decoder_q: bfloat16 [1408, 1408], P(None, 'section'), may hold values from -0.15625 to 0.15625
- decoder_kv: bfloat16 [1408, 2, 176], P(None, None, 'section'), may hold values from -0.15625 to 0.15625
- decoder_out: bfloat16 [1408, 1408], P('section'), may hold values from -0.875 to 0.875
Outputs:
- decoded: bfloat16 [256, 64, 1408], P(None, 'seq')
Inputs may be any that keep to these rules, and one draw needn't show every extreme that they name: `image_grid`: patch rows and columns are even, columns are 8 or 16; the images of one index of seq lie back to back and cover exactly its 512 patches. `image_offsets`: each image's first patch; images are in order, back to back, the first of an index of seq at its first patch. `dest_positions`: the 128 merged rows of one index of seq go, in order, to 128 consecutive prompt positions; the ranges of different indices do not meet. `segment_ids`: never falls along prompt positions; every document number is used.
All inputs are finite; a program needn't handle non-finite values.
Results may differ from a plain program's by a relative error of at most 0.025.
Values may be sent and summed in bfloat16 or wider, within the bound.
No kernel may reach another device: no remote copies, remote signals or barrier semaphores. Data moves between devices by JAX's collectives and lax.ppermute only.
A program may use at most 128 MiB of HBM per device.

v0:
```python
import math
import jax
import jax.numpy as jnp
from jax import lax
from jax.sharding import PartitionSpec as P

D = 1408
HEAD = 88
CHUNKS = 4


def layer_norm(values):
    values = values.astype(jnp.float32)
    centred = values - jnp.mean(values, -1, keepdims=True)
    return centred * lax.rsqrt(jnp.mean(centred * centred, -1, keepdims=True) + 1e-06)


def root_norm(values):
    values = values.astype(jnp.float32)
    return values * lax.rsqrt(jnp.mean(values * values, -1, keepdims=True) + 1e-06)


def merge_rows(grid, offsets, count):
    heights = grid[:, 0]
    widths = grid[:, 1]
    group_start = offsets // 4
    group_count = heights * widths // 4
    merged_ids = jnp.arange(count, dtype=jnp.int32)
    inside = (
        (merged_ids[:, None] >= group_start[None, :])
        & (merged_ids[:, None] < (group_start + group_count)[None, :])
    ).astype(jnp.int32)
    first_group = jnp.sum(inside * group_start[None, :], 1)
    first_patch = jnp.sum(inside * offsets[None, :], 1)
    row_width = jnp.sum(inside * widths[None, :], 1)
    within = merged_ids - first_group
    groups_across = row_width // 2
    group_row = within // groups_across
    group_col = within % groups_across
    corner = first_patch + 2 * group_row * row_width + 2 * group_col
    return jnp.stack([corner, corner + 1, corner + row_width, corner + row_width + 1], 1)


def swap(values):
    return lax.ppermute(values, "section", [(0, 1), (1, 0)])


def in_head_order(first, own, other, axis):
    return jnp.where(
        first, jnp.concatenate([own, other], axis), jnp.concatenate([other, own], axis)
    )


def body(
    patches,
    image_grid,
    image_offsets,
    dest_positions,
    text_embeds,
    segment_ids,
    vision_qkv,
    vision_out,
    projector,
    decoder_q,
    decoder_kv,
    decoder_out,
):
    section_index = lax.axis_index("section")
    seq_index = lax.axis_index("seq")
    seq_count = lax.axis_size("seq")
    first = section_index == 0
    scale = 3.0 / math.sqrt(HEAD)
    patch_count = patches.shape[0]
    local_heads = vision_out.shape[0] // HEAD
    merged_count = patch_count // 4
    vision_out_other = swap(vision_out)
    decoder_out_full = in_head_order(first, decoder_out, swap(decoder_out), 0)
    normed = layer_norm(patches).astype(jnp.bfloat16)
    mixed = jnp.dot(normed, vision_qkv.reshape(D, -1), preferred_element_type=jnp.float32).reshape(
        patch_count, 3, local_heads, HEAD
    )
    queries = root_norm(mixed[:, 0]).astype(jnp.bfloat16)
    keys = root_norm(mixed[:, 1]).astype(jnp.bfloat16)
    values = mixed[:, 2].astype(jnp.bfloat16)
    offsets = image_offsets - seq_index * patch_count
    image_of = jnp.sum(
        (jnp.arange(patch_count, dtype=jnp.int32)[:, None] >= offsets[None, :]).astype(jnp.int32), 1
    )
    scores = jnp.einsum("qhd,khd->hqk", queries, keys, preferred_element_type=jnp.float32) * scale
    same = (image_of[:, None] == image_of[None, :])[None]
    weights = jnp.where(same, jnp.exp(scores), jnp.zeros_like(scores))
    totals = jnp.sum(weights, -1)
    mixed_values = jnp.einsum(
        "hqk,khd->qhd", weights.astype(jnp.bfloat16), values, preferred_element_type=jnp.float32
    )
    attended = (
        (mixed_values / jnp.transpose(totals)[:, :, None])
        .astype(jnp.bfloat16)
        .reshape(patch_count, local_heads * HEAD)
    )
    picks = merge_rows(image_grid, offsets, merged_count)
    own_picks = lax.dynamic_slice_in_dim(picks, 2 * section_index, 2, 1).reshape(-1)
    other_picks = lax.dynamic_slice_in_dim(picks, 2 - 2 * section_index, 2, 1).reshape(-1)
    received_heads = swap(attended[other_picks])
    own_rows = jnp.concatenate([attended[own_picks], received_heads], 1)
    full_out = jnp.concatenate([vision_out, vision_out_other], 0)
    kept = (
        patches[own_picks].astype(jnp.float32)
        + jnp.dot(own_rows, full_out, preferred_element_type=jnp.float32)
    ).astype(jnp.bfloat16)
    merge_terms = jnp.dot(
        kept.reshape(merged_count, 2 * D),
        projector.reshape(2 * D, D),
        preferred_element_type=jnp.float32,
    )
    image_rows = (merge_terms + swap(merge_terms)).astype(jnp.bfloat16)
    per_peer = merged_count // seq_count
    run_starts = dest_positions.reshape(seq_count, merged_count)[:, 0]
    own_start = run_starts[seq_index]
    received = lax.all_to_all(
        jnp.roll(image_rows.reshape(per_peer, seq_count, image_rows.shape[1]), own_start, axis=1),
        "seq",
        split_axis=1,
        concat_axis=1,
        tiled=True,
    )
    slot_base = jnp.arange(per_peer, dtype=jnp.int32)[:, None] * seq_count
    landing = (
        run_starts[None, :] + slot_base + (seq_index - run_starts[None, :]) % seq_count
    ) // seq_count
    text_rows = text_embeds.shape[0]
    prompt = text_embeds.reshape(text_rows, D).at[landing.reshape(-1)].set(received.reshape(-1, D))
    text_normed = root_norm(prompt).astype(jnp.bfloat16)
    text_queries = root_norm(
        jnp.dot(text_normed, decoder_q, preferred_element_type=jnp.float32).reshape(
            text_rows, local_heads, HEAD
        )
    ).astype(jnp.bfloat16)
    paired = jnp.dot(
        text_normed, decoder_kv.reshape(D, -1), preferred_element_type=jnp.float32
    ).reshape(text_rows, 2, HEAD)
    key_rows = root_norm(paired[:, 0]).astype(jnp.bfloat16)
    value_rows = paired[:, 1].astype(jnp.bfloat16)
    shared = jnp.stack([key_rows, value_rows], 1)
    query_places = jnp.arange(text_rows, dtype=jnp.int32) * seq_count + seq_index
    query_segments = lax.dynamic_slice_in_dim(segment_ids, seq_index, 1, 1)[:, 0]
    step = text_rows // CHUNKS
    sums = jnp.zeros((text_rows, local_heads, HEAD), jnp.float32)
    totals = jnp.zeros((text_rows, local_heads), jnp.float32)
    for chunk in range(CHUNKS):
        low = chunk * step
        piece = lax.all_gather(shared[None, low : low + step], "seq", axis=0, tiled=True)
        piece = piece.reshape(seq_count * step, 2, HEAD)
        key_places = (
            jnp.arange(seq_count, dtype=jnp.int32)[:, None]
            + (low + jnp.arange(step, dtype=jnp.int32))[None, :] * seq_count
        ).reshape(-1)
        key_segments = jnp.transpose(segment_ids[low : low + step]).reshape(-1)
        chunk_queries = text_queries[low:]
        scores = (
            jnp.einsum(
                "qgd,ld->qgl", chunk_queries, piece[:, 0], preferred_element_type=jnp.float32
            )
            * scale
        )
        allowed = (key_places[None, :] <= query_places[low:, None]) & (
            key_segments[None, :] == query_segments[low:, None]
        )
        weights = jnp.where(allowed[:, None, :], jnp.exp(scores), jnp.zeros_like(scores))
        totals = totals.at[low:].add(jnp.sum(weights, -1))
        sums = sums.at[low:].add(
            jnp.einsum(
                "qgl,ld->qgd",
                weights.astype(jnp.bfloat16),
                piece[:, 1],
                preferred_element_type=jnp.float32,
            )
        )
    attended_text = (sums / totals[..., None]).astype(jnp.bfloat16).reshape(text_rows, -1)
    all_heads = in_head_order(first, attended_text, swap(attended_text), 1)
    output_terms = jnp.dot(all_heads, decoder_out_full, preferred_element_type=jnp.float32)
    decoded = (prompt.astype(jnp.float32) + output_terms).astype(jnp.bfloat16)
    return decoded.reshape(text_rows, 1, D)


def solution(mesh):
    placed = (
        P("seq", None),
        P("seq", None),
        P("seq"),
        P(),
        P(None, "seq", None),
        P(),
        P(None, None, "section"),
        P("section", None),
        P("section", None, None),
        P(None, "section"),
        P(None, None, "section"),
        P("section", None),
    )
    return jax.shard_map(
        body, mesh=mesh, in_specs=placed, out_specs=P(None, "seq", None), check_vma=False
    )
```

profile of v0, /device:TPU:1, one launch (start us, length us, event | category | flops | bytes accessed | tf_op | source)
XLA Modules:
  0.0 394.0 jit_solution(17752541069491407956)
XLA Ops:
  12.8 6.0 %fusion.57 = f32[512,3,8,88]{0,3,2,1:T(8,128)S(1)} fusion(bf16[3,8,88,1408]{3,2,1,0:T(8,128)(2,1)} %bitcast.178, bf16[512,1408]{1,0:T(8,128)(2,1)S(1)} %copy-done.2, f32[512]{0:T(512)S(1)} %add_rsqrt_fusion.3, f32[512]{0:T(512)S(1)} %broadcast_multiply_fusion), kind=kOutput, calls=%fused_computation.63 | convolution fusion | flops 3047948288 | bytes 11718656 | tf_op jit(solution)/shard_map/dot_general | solution.py:79
  21.8 4.2 %fusion.15 = (f32[8,512]{1,0:T(8,128)S(1)}, f32[8,512,512]{1,2,0:T(8,128)S(1)}) fusion(pred[512,512]{0,1:T(8,128)(4,1)} %broadcast_compare_fusion, f32[512,3,8,88]{0,3,2,1:T(8,128)} %copy-done.4, f32[512,8]{0,1:T(8,128)S(1)} %get-tuple-element.165, f32[512,8]{0,1:T(8,128)S(1)} %get-tuple-element.166), kind=kOutput, calls=%fused_computation.21 | convolution fusion | flops 376827904 | bytes 11583488 | tf_op jit(solution)/shard_map/qhd,khd->hqk/dot_general | solution.py:89
  26.1 3.1 divide_convert_fusion
  31.1 4.3 %gather_fusion = bf16[256,1408]{1,0:T(8,128)(2,1)} fusion(bf16[512,1408]{1,0:T(8,128)(2,1)} %param.32, s32[1024]{0:T(1024)S(1)} %pad_clamp_fusion.1), kind=kCustom, calls=%fused_computation | custom fusion | bytes 1442816 | tf_op jit(solution)/shard_map/gather | solution.py:108
  37.3 4.0 %fusion.46 = bf16[256,1408]{1,0:T(8,128)(2,1)S(1)} fusion(bf16[704,1408]{1,0:T(8,128)(2,1)} %collective-permute-done.1, bf16[704,1408]{1,0:T(8,128)(2,1)} %param.39, bf16[256,1408]{1,0:T(8,128)(2,1)} %gather_fusion, bf16[256,704]{1,0:T(8,128)(2,1)} %collective-permute-done, bf16[256,704]{1,0:T(8,128)(2,1)} %gather_fusion.1), kind=kOutput, calls=%fused_computation.53 | convolution fusion | flops 1025474560 | bytes 6127616 | tf_op jit(solution)/shard_map/dot_general | solution.py:109
  41.6 4.5 %fusion.128 = f32[128,1408]{1,0:T(8,128)S(1)} fusion(bf16[128,2816]{1,0:T(8,128)(2,1)S(1)} %reshape.1031, bf16[2816,1408]{1,0:T(8,128)(2,1)} %bitcast.163), kind=kOutput, calls=%fused_computation.233 | convolution fusion | flops 1015021568 | bytes 9371648 | tf_op jit(solution)/shard_map/dot_general | solution.py:111
  52.4 11.2 %all-to-all-start = ((bf16[2,64,1408]{2,0,1:T(2,128)(2,1)}), bf16[2,64,1408]{2,0,1:T(2,128)(2,1)S(1)}, u32[]{:S(2)}, u32[]{:S(2)}) async-start(bf16[2,64,1408]{2,0,1:T(2,128)(2,1)} %fusion.96), calls=%async_computation | async-start | bytes 720896 | tf_op jit(solution)/shard_map/all_to_all | solution.py:120
  63.9 10.6 %all-to-all-done = bf16[2,64,1408]{2,0,1:T(2,128)(2,1)S(1)} async-done(((bf16[2,64,1408]{2,0,1:T(2,128)(2,1)}), bf16[2,64,1408]{2,0,1:T(2,128)(2,1)S(1)}, u32[]{:S(2)}, u32[]{:S(2)}) %all-to-all-start) | async-done | bytes 360480 | tf_op jit(solution)/shard_map/all_to_all | solution.py:120
  92.6 48.0 %all-gather.9.cloned.1.call-done = bf16[4096,2,88]{2,1,0:T(2,128)(2,1)} async-done(((bf16[64,2,88]{2,1,0:T(2,128)(2,1)}), bf16[4096,2,88]{2,1,0:T(2,128)(2,1)}) %all-gather.9.cloned.1.call-update) | async-done | bytes 1441808 | tf_op jit(solution)/shard_map/all_gather | solution.py:152
  140.6 7.2 %fusion.126 = (bf16[4096,1,88]{2,1,0:T(2,128)(2,1)}, bf16[4096,1,88]{2,1,0:T(2,128)(2,1)}) fusion(bf16[4096,2,88]{2,1,0:T(2,128)(2,1)} %all-gather.9.cloned.1.call-done), kind=kLoop, calls=%fused_computation.231 | loop fusion | bytes 2883584 | tf_op jit(solution)/shard_map/slice | solution.py:175
  147.8 5.3 %copy.126 = bf16[4096,1,88]{0,2,1:T(8,128)(2,1)} copy(bf16[4096,1,88]{2,1,0:T(2,128)(2,1)} %get-tuple-element.138) | data formatting | bytes 1441792
  153.0 5.3 %copy.127 = bf16[4096,1,88]{0,2,1:T(8,128)(2,1)} copy(bf16[4096,1,88]{2,1,0:T(2,128)(2,1)} %get-tuple-element.137) | data formatting | bytes 1441792
  158.3 48.3 %all-gather.11.cloned.1.call-done = bf16[4096,2,88]{2,1,0:T(2,128)(2,1)} async-done(((bf16[64,2,88]{2,1,0:T(2,128)(2,1)}), bf16[4096,2,88]{2,1,0:T(2,128)(2,1)}) %all-gather.11.cloned.1.call-update) | async-done | bytes 1441808 | tf_op jit(solution)/shard_map/all_gather | solution.py:152
  206.6 6.9 %fusion.125 = (bf16[4096,1,88]{2,1,0:T(2,128)(2,1)}, bf16[4096,1,88]{2,1,0:T(2,128)(2,1)}) fusion(bf16[4096,2,88]{2,1,0:T(2,128)(2,1)} %all-gather.11.cloned.1.call-done), kind=kLoop, calls=%fused_computation.230 | loop fusion | bytes 2883584 | tf_op jit(solution)/shard_map/slice | solution.py:175
  213.5 4.7 %copy.128 = bf16[4096,1,88]{0,2,1:T(8,128)(2,1)S(1)} copy(bf16[4096,1,88]{2,1,0:T(2,128)(2,1)} %get-tuple-element.136) | data formatting | bytes 1441792
  218.2 5.3 %copy.129 = bf16[4096,1,88]{0,2,1:T(8,128)(2,1)} copy(bf16[4096,1,88]{2,1,0:T(2,128)(2,1)} %get-tuple-element.135) | data formatting | bytes 1441792
  223.5 12.1 %fusion.2 = (f32[192,8]{1,0:T(8,128)}, f32[192,8,4096]{2,1,0:T(8,128)}) fusion(pred[192,4096]{1,0:T(8,128)(4,1)S(1)} %copy-done.7, bf16[256,8,88]{2,1,0:T(8,128)(2,1)S(1)} %multiply_convert_fusion.2, bf16[4096,1,88]{0,2,1:T(8,128)(2,1)S(1)} %copy.128), kind=kOutput, calls=%fused_computation.8 | convolution fusion | flops 1126169088 | bytes 27039744 | tf_op jit(solution)/shard_map/qgd,ld->qgl/dot_general | solution.py:161
  235.6 10.5 %fusion.9 = f32[192,8,88]{2,1,0:T(8,128)S(1)} fusion(f32[192,8,4096]{2,1,0:T(8,128)} %get-tuple-element.158, pred[192,4096]{1,0:T(8,128)(4,1)S(1)} %copy-done.7, bf16[4096,1,88]{0,2,1:T(8,128)(2,1)} %copy.129), kind=kOutput, calls=%fused_computation.15 | convolution fusion | flops 1126170624 | bytes 27213824 | tf_op jit(solution)/shard_map/qgl,ld->qgd/dot_general | solution.py:172
  246.5 16.5 %fusion = (f32[256,8]{0,1:T(8,128)S(1)}, f32[256,8,4096]{2,0,1:T(8,128)}) fusion(pred[256,4096]{1,0:T(8,128)(4,1)} %compare_and_fusion, bf16[256,8,88]{0,2,1:T(8,128)(2,1)} %bitcast.170, bf16[4096,1,88]{0,2,1:T(8,128)(2,1)} %copy.126), kind=kOutput, calls=%fused_computation.5 | convolution fusion | flops 1501558784 | bytes 35692544 | tf_op jit(solution)/shard_map/qgd,ld->qgl/dot_general | solution.py:161
  263.0 13.8 %fusion.4 = f32[256,8,88]{0,2,1:T(8,128)S(1)} fusion(f32[256,8,4096]{2,0,1:T(8,128)} %get-tuple-element.156, pred[256,4096]{1,0:T(8,128)(4,1)S(1)} %copy-done.6, bf16[4096,1,88]{0,2,1:T(8,128)(2,1)S(1)} %copy-done.9), kind=kOutput, calls=%fused_computation.11 | convolution fusion | flops 1501560832 | bytes 36044800 | tf_op jit(solution)/shard_map/qgl,ld->qgd/dot_general | solution.py:172
  277.1 7.1 %scatter-add.20 = f32[256,8,88]{0,2,1:T(8,128)S(1)} dynamic-update-slice(f32[256,8,88]{0,2,1:T(8,128)S(1)} %fusion.4, f32[192,8,88]{0,2,1:T(8,128)S(1)} %slice_add_fusion, s32[]{:T(128)} %constant.358.clone.1, s32[]{:T(128)} %constant.360.clone.1, s32[]{:T(128)} %constant.360.clone.1) | dynamic-update-slice | bytes 1081348 | tf_op jit(solution)/shard_map/scatter-add | solution.py:171
  284.2 7.0 %fusion.124 = (bf16[4096,1,88]{2,1,0:T(2,128)(2,1)}, bf16[4096,1,88]{2,1,0:T(2,128)(2,1)}) fusion(bf16[4096,2,88]{2,1,0:T(2,128)(2,1)} %all-gather.13.cloned.1.call-done), kind=kLoop, calls=%fused_computation.229 | loop fusion | bytes 2883584 | tf_op jit(solution)/shard_map/slice | solution.py:175
  291.2 5.3 %copy.131 = bf16[4096,1,88]{0,2,1:T(8,128)(2,1)} copy(bf16[4096,1,88]{2,1,0:T(2,128)(2,1)} %get-tuple-element.133) | data formatting | bytes 1441792
  296.4 5.3 %copy.130 = bf16[4096,1,88]{0,2,1:T(8,128)(2,1)} copy(bf16[4096,1,88]{2,1,0:T(2,128)(2,1)} %get-tuple-element.134) | data formatting | bytes 1441792
  301.8 36.9 %all-gather.15.cloned.1.call-done = bf16[4096,2,88]{2,1,0:T(2,128)(2,1)} async-done(((bf16[64,2,88]{2,1,0:T(2,128)(2,1)}), bf16[4096,2,88]{2,1,0:T(2,128)(2,1)}) %all-gather.15.cloned.1.call-update) | async-done | bytes 1441808 | tf_op jit(solution)/shard_map/all_gather | solution.py:152
  338.7 6.8 %fusion.123 = (bf16[4096,1,88]{2,1,0:T(2,128)(2,1)}, bf16[4096,1,88]{2,1,0:T(2,128)(2,1)}) fusion(bf16[4096,2,88]{2,1,0:T(2,128)(2,1)} %all-gather.15.cloned.1.call-done), kind=kLoop, calls=%fused_computation.228 | loop fusion | bytes 2883584 | tf_op jit(solution)/shard_map/slice | solution.py:175
  345.5 4.6 %copy.132 = bf16[4096,1,88]{0,2,1:T(8,128)(2,1)S(1)} copy(bf16[4096,1,88]{2,1,0:T(2,128)(2,1)} %get-tuple-element.132) | data formatting | bytes 1441792
  350.1 5.3 %copy.133 = bf16[4096,1,88]{0,2,1:T(8,128)(2,1)} copy(bf16[4096,1,88]{2,1,0:T(2,128)(2,1)} %get-tuple-element.131) | data formatting | bytes 1441792
  355.4 3.9 fusion.17
  363.4 5.7 %fusion.7 = (f32[128,8]{0,1:T(8,128)S(1)}, f32[128,8,4096]{2,0,1:T(8,128)S(1)}) fusion(pred[128,4096]{1,0:T(8,128)(4,1)S(1)} %copy-done.11, bf16[4096,1,88]{0,2,1:T(8,128)(2,1)} %copy.130, bf16[128,8,88]{2,1,0:T(8,128)(2,1)S(1)} %slice-done), kind=kOutput, calls=%fused_computation.13 | convolution fusion | flops 750779392 | bytes 18206720 | tf_op jit(solution)/shard_map/qgd,ld->qgl/dot_general | solution.py:161
  372.2 5.0 %scatter-add.24 = f32[256,8,88]{0,2,1:T(8,128)S(1)} dynamic-update-slice(f32[256,8,88]{0,2,1:T(8,128)S(1)} %get-tuple-element.153, f32[64,8,88]{0,2,1:T(8,128)S(1)} %slice_add_fusion.1, s32[]{:T(128)} %constant.377.clone.1, s32[]{:T(128)} %constant.360.clone.1, s32[]{:T(128)} %constant.360.clone.1) | dynamic-update-slice | bytes 360452 | tf_op jit(solution)/shard_map/scatter-add | solution.py:171
  381.3 6.0 %fusion.50 = bf16[256,1,1408]{2,0,1:T(8,128)(2,1)} fusion(bf16[704,1408]{1,0:T(8,128)(2,1)} %collective-permute-done.4, bf16[704,1408]{1,0:T(8,128)(2,1)} %param.43, pred[]{:T(512)S(6)} %eq.136, bf16[256,1408]{1,0:T(8,128)(2,1)S(1)} %scatter_fusion, bf16[256,704]{0,1:T(8,128)(2,1)S(1)} %collective-permute-done.3, bf16[256,704]{0,1:T(8,128)(2,1)} %bitcast.172), kind=kOutput, calls=%fused_computation.55 | convolution fusion | flops 1037189120 | bytes 6127617 | tf_op jit(solution)/shard_map/dot_general | solution.py:181
  (157 shorter events, 47.4 us)
Async XLA Ops:
  6.5 82.6 %copy-start = (bf16[1408,704]{0,1:T(8,128)(2,1)S(1)}, bf16[1408,704]{0,1:T(8,128)(2,1)}, u32[]{:S(2)}) copy-start(bf16[1408,704]{0,1:T(8,128)(2,1)} %param.41) | copy-start | bytes 5947396
  6.5 5.8 %copy-start.2 = (bf16[512,1408]{1,0:T(8,128)(2,1)S(1)}, bf16[512,1408]{1,0:T(8,128)(2,1)}, u32[]{:S(2)}) copy-start(bf16[512,1408]{1,0:T(8,128)(2,1)} %param.32) | copy-start | bytes 4325380
  6.5 30.8 %collective-permute-start.1 = (bf16[704,1408]{1,0:T(8,128)(2,1)}, bf16[704,1408]{1,0:T(8,128)(2,1)}, u32[]{:S(2)}, u32[]{:S(2)}) collective-permute-start(bf16[704,1408]{1,0:T(8,128)(2,1)} %param.39), channel_id=1, source_target_pairs={{0,64},{64,0},{1,65},{65,1},{2,66},{66,2},{3,67},{67,3},{4,68},{68... | collective-permute-start | bytes 5947400 | tf_op jit(solution)/shard_map/ppermute | solution.py:45
  18.8 2.0 copy-start.4
  21.8 4.2 %copy-start.15 = (pred[512,512]{0,1:T(8,128)(4,1)S(1)}, pred[512,512]{0,1:T(8,128)(4,1)}, u32[]{:S(2)}) copy-start(pred[512,512]{0,1:T(8,128)(4,1)} %broadcast_compare_fusion) | copy-start | bytes 786436
  30.7 6.6 %collective-permute-start = (bf16[256,704]{1,0:T(8,128)(2,1)S(1)}, bf16[256,704]{1,0:T(8,128)(2,1)}, u32[]{:S(2)}, u32[]{:S(2)}) collective-permute-start(bf16[256,704]{1,0:T(8,128)(2,1)S(1)} %gather_fusion.2), channel_id=1, source_target_pairs={{0,64},{64,0},{1,65},{65,1},{2,66},{66,2},{3,67},{67,3},{4,68},{68... | collective-permute-start | bytes 1081352 | tf_op jit(solution)/shard_map/ppermute | solution.py:45
  41.5 5.0 %copy-start.17 = (s32[8192]{0:T(1024)S(1)}, s32[8192]{0:T(1024)}, u32[]{:S(2)}) copy-start(s32[8192]{0:T(1024)} %param.35) | copy-start | bytes 98308
  46.1 28.4 %copy-start.3 = (bf16[256,1,1408]{2,0,1:T(8,128)(2,1)S(1)}, bf16[256,1,1408]{2,0,1:T(8,128)(2,1)}, u32[]{:S(2)}) copy-start(bf16[256,1,1408]{2,0,1:T(8,128)(2,1)} %param.36) | copy-start | bytes 2162692
  46.1 3.0 collective-permute-start.2
  52.4 22.1 %all-to-all-start = ((bf16[2,64,1408]{2,0,1:T(2,128)(2,1)}), bf16[2,64,1408]{2,0,1:T(2,128)(2,1)S(1)}, u32[]{:S(2)}, u32[]{:S(2)}) async-start(bf16[2,64,1408]{2,0,1:T(2,128)(2,1)} %fusion.96), calls=%async_computation | async-start | bytes 720896 | tf_op jit(solution)/shard_map/all_to_all | solution.py:120
  63.6 76.9 %all-gather.9.cloned.1.call-start = ((), (), s32[]{:S(2)}) async-start(), calls=%async_computation.1 | async-start | bytes 2129920 | tf_op jit(solution)/shard_map/all_gather | solution.py:152
  74.5 6.1 %copy-start.13 = (s32[256,64]{0,1:T(8,128)S(1)}, s32[256,64]{0,1:T(8,128)}, u32[]{:S(2)}) copy-start(s32[256,64]{0,1:T(8,128)} %param.37) | copy-start | bytes 196612
  78.8 127.9 %all-gather.11.cloned.1.call-start = ((), (), s32[]{:S(2)}) async-start(), calls=%async_computation.2 | async-start | bytes 2129920 | tf_op jit(solution)/shard_map/all_gather | solution.py:152
  78.8 301.1 %collective-permute-start.4 = (bf16[704,1408]{1,0:T(8,128)(2,1)}, bf16[704,1408]{1,0:T(8,128)(2,1)}, u32[]{:S(2)}, u32[]{:S(2)}) collective-permute-start(bf16[704,1408]{1,0:T(8,128)(2,1)} %param.43), channel_id=1, source_target_pairs={{0,64},{64,0},{1,65},{65,1},{2,66},{66,2},{3,67},{67,3},{4,68},{68... | collective-permute-start | bytes 5947400 | tf_op jit(solution)/shard_map/ppermute | solution.py:45
  81.7 202.5 %all-gather.13.cloned.1.call-start = ((), (), s32[]{:S(2)}) async-start(), calls=%async_computation.3 | async-start | bytes 2129920 | tf_op jit(solution)/shard_map/all_gather | solution.py:152
  85.0 253.6 %all-gather.15.cloned.1.call-start = ((), (), s32[]{:S(2)}) async-start(), calls=%async_computation.4 | async-start | bytes 2129920 | tf_op jit(solution)/shard_map/all_gather | solution.py:152
  91.7 263.7 %copy-start.5 = (bf16[256,8,88]{2,1,0:T(8,128)(2,1)}, bf16[256,8,88]{2,1,0:T(8,128)(2,1)S(1)}, u32[]{:S(2)}) copy-start(bf16[256,8,88]{2,1,0:T(8,128)(2,1)S(1)} %multiply_convert_fusion.2) | copy-start | bytes 1081348
  213.5 10.0 %copy-start.7 = (pred[192,4096]{1,0:T(8,128)(4,1)S(1)}, pred[192,4096]{1,0:T(8,128)(4,1)}, u32[]{:S(2)}) copy-start(pred[192,4096]{1,0:T(8,128)(4,1)} %compare_and_fusion.1) | copy-start | bytes 2359300
  246.5 16.5 %copy-start.6 = (pred[256,4096]{1,0:T(8,128)(4,1)S(1)}, pred[256,4096]{1,0:T(8,128)(4,1)}, u32[]{:S(2)}) copy-start(pred[256,4096]{1,0:T(8,128)(4,1)} %compare_and_fusion) | copy-start | bytes 3145732
  246.5 16.5 %copy-start.9 = (bf16[4096,1,88]{0,2,1:T(8,128)(2,1)S(1)}, bf16[4096,1,88]{0,2,1:T(8,128)(2,1)}, u32[]{:S(2)}) copy-start(bf16[4096,1,88]{0,2,1:T(8,128)(2,1)} %copy.127) | copy-start | bytes 2162692
  355.4 3.9 copy-start.10
  355.4 3.9 copy-start.14
  359.3 3.7 copy-start.16
  359.3 4.1 %slice-start = ((bf16[256,8,88]{2,1,0:T(8,128)(2,1)}), bf16[128,8,88]{2,1,0:T(8,128)(2,1)S(1)}, s32[]{:S(2)}) async-start(bf16[256,8,88]{2,1,0:T(8,128)(2,1)} %copy-done.5), calls=%async_computation.5 | async-start | bytes 524288 | tf_op jit(solution)/shard_map/slice | solution.py:159
  359.3 4.1 %copy-start.11 = (pred[128,4096]{1,0:T(8,128)(4,1)S(1)}, pred[128,4096]{1,0:T(8,128)(4,1)}, u32[]{:S(2)}) copy-start(pred[128,4096]{1,0:T(8,128)(4,1)} %compare_and_fusion.2) | copy-start | bytes 1572868
  363.4 5.7 %copy-start.8 = (bf16[4096,1,88]{0,2,1:T(8,128)(2,1)S(1)}, bf16[4096,1,88]{0,2,1:T(8,128)(2,1)}, u32[]{:S(2)}) copy-start(bf16[4096,1,88]{0,2,1:T(8,128)(2,1)} %copy.131) | copy-start | bytes 2162692
  377.6 0.7 copy-start.12
  378.3 2.9 collective-permute-start.3
  381.3 6.0 %copy-start.1 = (bf16[1408,704]{0,1:T(8,128)(2,1)S(1)}, bf16[1408,704]{0,1:T(8,128)(2,1)}, u32[]{:S(2)}) copy-start(bf16[1408,704]{0,1:T(8,128)(2,1)} %param.41) | copy-start | bytes 5947396
Sparse Core Ops, SparseCore 0:
  78.9 61.6 all-gather.8
  143.4 63.1 all-gather.10
  209.5 63.1 all-gather.12
  275.4 63.1 all-gather.14
where the time goes:
time: 401 us; the launch traced here: 394 us
  waiting for transfers between devices  145 us (36%)
  local copies, waits for them, and re-layouts  102 us (25%)
  matrix products  98 us (24%)
  starting transfers between devices  17 us (4%)
  between operations  15.9 us (4%)
  other arithmetic  15.7 us (4%)
    all_gather x4, waiting for transfers between devices, body(): lax.all_gather(shared[None, low:low + step], 'seq', axis=0, tiled=True)  133 us
    unnamed x44, local copies, waits for them, and re-layouts  43.9 us
    dot_general x4, matrix products, body(): jnp.einsum('qgd,ld->qgl', chunk_queries, piece[:, 0], preferred_element_t...  38.2 us
    dot_general x4, matrix products, body(): jnp.einsum('qgl,ld->qgd', weights.astype(jnp.bfloat16), piece[:, 1], pref...  29.7 us
    slice x4, local copies, waits for them, and re-layouts, body(): piece[:, 1]  27.8 us
    scatter-add x2, local copies, waits for them, and re-layouts, body(): sums.at[low:]  12.1 us
    all_to_all x1, starting transfers between devices, body(): lax.all_to_all(jnp.roll(image_rows.reshape(per_peer, seq_count, image_row...  11.2 us
    all_to_all x1, waiting for transfers between devices, body(): lax.all_to_all(jnp.roll(image_rows.reshape(per_peer, seq_count, image_row...  10.6 us
  transfers between devices with their start and end apart: 10, of which 5 were waited for; matrix products, arithmetic and copies ran while one was open for 48% of the time, Pallas kernels for 0%

commit v1 on v0

--- a/solution.py
+++ b/solution.py
@@ -117,12 +117,24 @@
     per_peer = merged_count // seq_count
     run_starts = dest_positions.reshape(seq_count, merged_count)[:, 0]
     own_start = run_starts[seq_index]
-    received = lax.all_to_all(
-        jnp.roll(image_rows.reshape(per_peer, seq_count, image_rows.shape[1]), own_start, axis=1),
-        "seq",
-        split_axis=1,
-        concat_axis=1,
-        tiled=True,
+    received = jnp.concatenate(
+        lax.all_to_all(
+            jnp.stack(
+                jnp.split(
+                    jnp.roll(
+                        image_rows.reshape(per_peer, seq_count, image_rows.shape[1]),
+                        own_start,
+                        axis=1,
+                    ),
+                    lax.axis_size("seq"),
+                    axis=1,
+                )
+            ),
+            "seq",
+            0,
+            0,
+        ),
+        axis=1,
     )
     slot_base = jnp.arange(per_peer, dtype=jnp.int32)[:, None] * seq_count
     landing = (

time: 401 us -> 439 us (1.095)
  local copies, waits for them, and re-layouts: 102 us -> 140 us
    unnamed x44 -> x107, local copies, waits for them, and re-layouts: 43.9 us -> 81.6 us
  transfers between devices with their start and end apart: 10 -> 10, of which waited for: 5 -> 5; matrix products, arithmetic and copies ran while one was open for 48% -> 44% of each run, Pallas kernels for 0% -> 0%
where the time goes in v1:
time: 439 us; the launch traced here: 432 us
  waiting for transfers between devices  145 us (33%)
  local copies, waits for them, and re-layouts  140 us (32%)
  matrix products  98 us (22%)
  starting transfers between devices  17.4 us (4%)
  between operations  15.9 us (4%)
  other arithmetic  15 us (3%)
    all_gather x4, waiting for transfers between devices, body(): lax.all_gather(shared[None, low:low + step], 'seq', axis=0, tiled=True)  133 us
    unnamed x107, local copies, waits for them, and re-layouts  81.6 us
    dot_general x4, matrix products, body(): jnp.einsum('qgd,ld->qgl', chunk_queries, piece[:, 0], preferred_element_t...  38.2 us
    dot_general x4, matrix products, body(): jnp.einsum('qgl,ld->qgd', weights.astype(jnp.bfloat16), piece[:, 1], pref...  29.7 us
    slice x4, local copies, waits for them, and re-layouts, body(): piece[:, 1]  27.4 us
    scatter-add x2, local copies, waits for them, and re-layouts, body(): sums.at[low:]  12.1 us
    all_to_all x1, starting transfers between devices, body(): lax.all_to_all(jnp.stack(jnp.split(jnp.roll(image_rows.reshape(per_peer,...  11.2 us
    all_to_all x1, waiting for transfers between devices, body(): lax.all_to_all(jnp.stack(jnp.split(jnp.roll(image_rows.reshape(per_peer,...  10.6 us
  transfers between devices with their start and end apart: 10, of which 5 were waited for; matrix products, arithmetic and copies ran while one was open for 44% of the time, Pallas kernels for 0%

profile of v1, /device:TPU:1, one launch (start us, length us, event | category | flops | bytes accessed | tf_op | source)
XLA Modules:
  0.0 431.6 jit_solution(17339814584571348226)
XLA Ops:
  12.8 6.0 %fusion.57 = f32[512,3,8,88]{0,3,2,1:T(8,128)S(1)} fusion(bf16[3,8,88,1408]{3,2,1,0:T(8,128)(2,1)} %bitcast.436, bf16[512,1408]{1,0:T(8,128)(2,1)S(1)} %copy-done.2, f32[512]{0:T(512)S(1)} %add_rsqrt_fusion.3, f32[512]{0:T(512)S(1)} %broadcast_multiply_fusion), kind=kOutput, calls=%fused_computation.63 | convolution fusion | flops 3047948288 | bytes 11718656 | tf_op jit(solution)/shard_map/dot_general | solution.py:79
  21.8 4.2 fusion.15
  26.1 3.1 divide_convert_fusion
  31.1 4.3 gather_fusion
  37.3 4.0 fusion.46
  41.6 4.5 %fusion.128 = f32[128,1408]{1,0:T(8,128)S(1)} fusion(bf16[128,2816]{1,0:T(8,128)(2,1)S(1)} %reshape.1031, bf16[2816,1408]{1,0:T(8,128)(2,1)} %bitcast.420), kind=kOutput, calls=%fused_computation.361 | convolution fusion | flops 1015021568 | bytes 9371648 | tf_op jit(solution)/shard_map/dot_general | solution.py:111
  90.0 11.2 %all-to-all-start = ((bf16[64,2,1,1408]{3,1,2,0:T(2,128)(2,1)}), bf16[64,2,1,1408]{3,1,2,0:T(2,128)(2,1)S(1)}, u32[]{:S(2)}, u32[]{:S(2)}) async-start(bf16[64,2,1,1408]{3,1,2,0:T(2,128)(2,1)} %constant_dynamic-update-slice_fusion), calls=%async_computation | async-start | bytes 720896 | tf_op jit(solution)/shard_map/all_to_all | solution.py:121
  101.5 10.6 %all-to-all-done = bf16[64,2,1,1408]{3,1,2,0:T(2,128)(2,1)S(1)} async-done(((bf16[64,2,1,1408]{3,1,2,0:T(2,128)(2,1)}), bf16[64,2,1,1408]{3,1,2,0:T(2,128)(2,1)S(1)}, u32[]{:S(2)}, u32[]{:S(2)}) %all-to-all-start) | async-done | bytes 360480 | tf_op jit(solution)/shard_map/all_to_all | solution.py:121
  130.6 47.6 %all-gather.9.cloned.1.call-done = bf16[4096,2,88]{2,1,0:T(2,128)(2,1)} async-done(((bf16[64,2,88]{2,1,0:T(2,128)(2,1)}), bf16[4096,2,88]{2,1,0:T(2,128)(2,1)}) %all-gather.9.cloned.1.call-update) | async-done | bytes 1441808 | tf_op jit(solution)/shard_map/all_gather | solution.py:164
  178.1 6.8 %fusion.126 = (bf16[4096,1,88]{2,1,0:T(2,128)(2,1)}, bf16[4096,1,88]{2,1,0:T(2,128)(2,1)}) fusion(bf16[4096,2,88]{2,1,0:T(2,128)(2,1)} %all-gather.9.cloned.1.call-done), kind=kLoop, calls=%fused_computation.359 | loop fusion | bytes 2883584 | tf_op jit(solution)/shard_map/slice | solution.py:187
  185.0 5.3 %copy.196 = bf16[4096,1,88]{0,2,1:T(8,128)(2,1)} copy(bf16[4096,1,88]{2,1,0:T(2,128)(2,1)} %get-tuple-element.138) | data formatting | bytes 1441792
  190.2 5.3 %copy.197 = bf16[4096,1,88]{0,2,1:T(8,128)(2,1)} copy(bf16[4096,1,88]{2,1,0:T(2,128)(2,1)} %get-tuple-element.137) | data formatting | bytes 1441792
  195.5 48.7 %all-gather.11.cloned.1.call-done = bf16[4096,2,88]{2,1,0:T(2,128)(2,1)} async-done(((bf16[64,2,88]{2,1,0:T(2,128)(2,1)}), bf16[4096,2,88]{2,1,0:T(2,128)(2,1)}) %all-gather.11.cloned.1.call-update) | async-done | bytes 1441808 | tf_op jit(solution)/shard_map/all_gather | solution.py:164
  244.2 6.9 %fusion.125 = (bf16[4096,1,88]{2,1,0:T(2,128)(2,1)}, bf16[4096,1,88]{2,1,0:T(2,128)(2,1)}) fusion(bf16[4096,2,88]{2,1,0:T(2,128)(2,1)} %all-gather.11.cloned.1.call-done), kind=kLoop, calls=%fused_computation.358 | loop fusion | bytes 2883584 | tf_op jit(solution)/shard_map/slice | solution.py:187
  251.1 4.7 %copy.198 = bf16[4096,1,88]{0,2,1:T(8,128)(2,1)S(1)} copy(bf16[4096,1,88]{2,1,0:T(2,128)(2,1)} %get-tuple-element.136) | data formatting | bytes 1441792
  255.8 5.3 %copy.199 = bf16[4096,1,88]{0,2,1:T(8,128)(2,1)} copy(bf16[4096,1,88]{2,1,0:T(2,128)(2,1)} %get-tuple-element.135) | data formatting | bytes 1441792
  261.1 12.1 %fusion.2 = (f32[192,8]{1,0:T(8,128)}, f32[192,8,4096]{2,1,0:T(8,128)}) fusion(pred[192,4096]{1,0:T(8,128)(4,1)S(1)} %copy-done.7, bf16[256,8,88]{2,1,0:T(8,128)(2,1)S(1)} %multiply_convert_fusion.2, bf16[4096,1,88]{0,2,1:T(8,128)(2,1)S(1)} %copy.198), kind=kOutput, calls=%fused_computation.8 | convolution fusion | flops 1126169088 | bytes 27039744 | tf_op jit(solution)/shard_map/qgd,ld->qgl/dot_general | solution.py:173
  273.2 10.5 %fusion.9 = f32[192,8,88]{2,1,0:T(8,128)S(1)} fusion(f32[192,8,4096]{2,1,0:T(8,128)} %get-tuple-element.158, pred[192,4096]{1,0:T(8,128)(4,1)S(1)} %copy-done.7, bf16[4096,1,88]{0,2,1:T(8,128)(2,1)} %copy.199), kind=kOutput, calls=%fused_computation.15 | convolution fusion | flops 1126170624 | bytes 27213824 | tf_op jit(solution)/shard_map/qgl,ld->qgd/dot_general | solution.py:184
  284.1 16.5 %fusion = (f32[256,8]{0,1:T(8,128)S(1)}, f32[256,8,4096]{2,0,1:T(8,128)}) fusion(pred[256,4096]{1,0:T(8,128)(4,1)} %compare_and_fusion, bf16[256,8,88]{0,2,1:T(8,128)(2,1)} %bitcast.428, bf16[4096,1,88]{0,2,1:T(8,128)(2,1)} %copy.196), kind=kOutput, calls=%fused_computation.5 | convolution fusion | flops 1501558784 | bytes 35692544 | tf_op jit(solution)/shard_map/qgd,ld->qgl/dot_general | solution.py:173
  300.6 13.8 %fusion.4 = f32[256,8,88]{0,2,1:T(8,128)S(1)} fusion(f32[256,8,4096]{2,0,1:T(8,128)} %get-tuple-element.156, pred[256,4096]{1,0:T(8,128)(4,1)S(1)} %copy-done.6, bf16[4096,1,88]{0,2,1:T(8,128)(2,1)S(1)} %copy-done.9), kind=kOutput, calls=%fused_computation.11 | convolution fusion | flops 1501560832 | bytes 36044800 | tf_op jit(solution)/shard_map/qgl,ld->qgd/dot_general | solution.py:184
  314.7 7.1 %scatter-add.20 = f32[256,8,88]{0,2,1:T(8,128)S(1)} dynamic-update-slice(f32[256,8,88]{0,2,1:T(8,128)S(1)} %fusion.4, f32[192,8,88]{0,2,1:T(8,128)S(1)} %slice_add_fusion, s32[]{:T(128)} %constant.358.clone.1, s32[]{:T(128)} %constant.360.clone.1, s32[]{:T(128)} %constant.360.clone.1) | dynamic-update-slice | bytes 1081348 | tf_op jit(solution)/shard_map/scatter-add | solution.py:183
  321.8 7.0 %fusion.124 = (bf16[4096,1,88]{2,1,0:T(2,128)(2,1)}, bf16[4096,1,88]{2,1,0:T(2,128)(2,1)}) fusion(bf16[4096,2,88]{2,1,0:T(2,128)(2,1)} %all-gather.13.cloned.1.call-done), kind=kLoop, calls=%fused_computation.357 | loop fusion | bytes 2883584 | tf_op jit(solution)/shard_map/slice | solution.py:187
  328.8 5.3 %copy.201 = bf16[4096,1,88]{0,2,1:T(8,128)(2,1)} copy(bf16[4096,1,88]{2,1,0:T(2,128)(2,1)} %get-tuple-element.133) | data formatting | bytes 1441792
  334.0 5.3 %copy.200 = bf16[4096,1,88]{0,2,1:T(8,128)(2,1)} copy(bf16[4096,1,88]{2,1,0:T(2,128)(2,1)} %get-tuple-element.134) | data formatting | bytes 1441792
  339.4 36.9 %all-gather.15.cloned.1.call-done = bf16[4096,2,88]{2,1,0:T(2,128)(2,1)} async-done(((bf16[64,2,88]{2,1,0:T(2,128)(2,1)}), bf16[4096,2,88]{2,1,0:T(2,128)(2,1)}) %all-gather.15.cloned.1.call-update) | async-done | bytes 1441808 | tf_op jit(solution)/shard_map/all_gather | solution.py:164
  376.3 6.8 %fusion.123 = (bf16[4096,1,88]{2,1,0:T(2,128)(2,1)}, bf16[4096,1,88]{2,1,0:T(2,128)(2,1)}) fusion(bf16[4096,2,88]{2,1,0:T(2,128)(2,1)} %all-gather.15.cloned.1.call-done), kind=kLoop, calls=%fused_computation.356 | loop fusion | bytes 2883584 | tf_op jit(solution)/shard_map/slice | solution.py:187
  383.0 4.6 %copy.202 = bf16[4096,1,88]{0,2,1:T(8,128)(2,1)S(1)} copy(bf16[4096,1,88]{2,1,0:T(2,128)(2,1)} %get-tuple-element.132) | data formatting | bytes 1441792
  387.7 5.3 %copy.203 = bf16[4096,1,88]{0,2,1:T(8,128)(2,1)} copy(bf16[4096,1,88]{2,1,0:T(2,128)(2,1)} %get-tuple-element.131) | data formatting | bytes 1441792
  393.0 3.9 fusion.17
  401.0 5.7 %fusion.7 = (f32[128,8]{0,1:T(8,128)S(1)}, f32[128,8,4096]{2,0,1:T(8,128)S(1)}) fusion(pred[128,4096]{1,0:T(8,128)(4,1)S(1)} %copy-done.11, bf16[4096,1,88]{0,2,1:T(8,128)(2,1)} %copy.200, bf16[128,8,88]{2,1,0:T(8,128)(2,1)S(1)} %slice-done), kind=kOutput, calls=%fused_computation.13 | convolution fusion | flops 750779392 | bytes 18206720 | tf_op jit(solution)/shard_map/qgd,ld->qgl/dot_general | solution.py:173
  409.8 5.0 %scatter-add.24 = f32[256,8,88]{0,2,1:T(8,128)S(1)} dynamic-update-slice(f32[256,8,88]{0,2,1:T(8,128)S(1)} %get-tuple-element.153, f32[64,8,88]{0,2,1:T(8,128)S(1)} %slice_add_fusion.1, s32[]{:T(128)} %constant.377.clone.1, s32[]{:T(128)} %constant.360.clone.1, s32[]{:T(128)} %constant.360.clone.1) | dynamic-update-slice | bytes 360452 | tf_op jit(solution)/shard_map/scatter-add | solution.py:183
  418.9 6.0 %fusion.50 = bf16[256,1,1408]{2,0,1:T(8,128)(2,1)} fusion(bf16[704,1408]{1,0:T(8,128)(2,1)} %collective-permute-done.4, bf16[704,1408]{1,0:T(8,128)(2,1)} %param.43, pred[]{:T(512)S(6)} %eq.136, bf16[256,1408]{1,0:T(8,128)(2,1)S(1)} %scatter_fusion, bf16[256,704]{0,1:T(8,128)(2,1)S(1)} %collective-permute-done.3, bf16[256,704]{0,1:T(8,128)(2,1)} %bitcast.430), kind=kOutput, calls=%fused_computation.55 | convolution fusion | flops 1037189120 | bytes 6127617 | tf_op jit(solution)/shard_map/dot_general | solution.py:193
  (221 shorter events, 85.4 us)
Async XLA Ops:
  6.5 120.6 %copy-start = (bf16[1408,704]{0,1:T(8,128)(2,1)S(1)}, bf16[1408,704]{0,1:T(8,128)(2,1)}, u32[]{:S(2)}) copy-start(bf16[1408,704]{0,1:T(8,128)(2,1)} %param.41) | copy-start | bytes 5947396
  6.5 5.8 %copy-start.2 = (bf16[512,1408]{1,0:T(8,128)(2,1)S(1)}, bf16[512,1408]{1,0:T(8,128)(2,1)}, u32[]{:S(2)}) copy-start(bf16[512,1408]{1,0:T(8,128)(2,1)} %param.32) | copy-start | bytes 4325380
  6.5 30.8 %collective-permute-start.1 = (bf16[704,1408]{1,0:T(8,128)(2,1)}, bf16[704,1408]{1,0:T(8,128)(2,1)}, u32[]{:S(2)}, u32[]{:S(2)}) collective-permute-start(bf16[704,1408]{1,0:T(8,128)(2,1)} %param.39), channel_id=1, source_target_pairs={{0,64},{64,0},{1,65},{65,1},{2,66},{66,2},{3,67},{67,3},{4,68},{68... | collective-permute-start | bytes 5947400 | tf_op jit(solution)/shard_map/ppermute | solution.py:45
  18.8 2.0 copy-start.4
  21.8 4.2 copy-start.15
  30.7 6.6 %collective-permute-start = (bf16[256,704]{1,0:T(8,128)(2,1)S(1)}, bf16[256,704]{1,0:T(8,128)(2,1)}, u32[]{:S(2)}, u32[]{:S(2)}) collective-permute-start(bf16[256,704]{1,0:T(8,128)(2,1)S(1)} %gather_fusion.2), channel_id=1, source_target_pairs={{0,64},{64,0},{1,65},{65,1},{2,66},{66,2},{3,67},{67,3},{4,68},{68... | collective-permute-start | bytes 1081352 | tf_op jit(solution)/shard_map/ppermute | solution.py:45
  41.5 5.0 %copy-start.17 = (s32[8192]{0:T(1024)S(1)}, s32[8192]{0:T(1024)}, u32[]{:S(2)}) copy-start(s32[8192]{0:T(1024)} %param.35) | copy-start | bytes 98308
  46.1 66.0 %copy-start.3 = (bf16[256,1,1408]{2,0,1:T(8,128)(2,1)S(1)}, bf16[256,1,1408]{2,0,1:T(8,128)(2,1)}, u32[]{:S(2)}) copy-start(bf16[256,1,1408]{2,0,1:T(8,128)(2,1)} %param.36) | copy-start | bytes 2162692
  46.1 3.0 collective-permute-start.2
  90.0 22.1 %all-to-all-start = ((bf16[64,2,1,1408]{3,1,2,0:T(2,128)(2,1)}), bf16[64,2,1,1408]{3,1,2,0:T(2,128)(2,1)S(1)}, u32[]{:S(2)}, u32[]{:S(2)}) async-start(bf16[64,2,1,1408]{3,1,2,0:T(2,128)(2,1)} %constant_dynamic-update-slice_fusion), calls=%async_computation | async-start | bytes 720896 | tf_op jit(solution)/shard_map/all_to_all | solution.py:121
  101.2 76.9 %all-gather.9.cloned.1.call-start = ((), (), s32[]{:S(2)}) async-start(), calls=%async_computation.1 | async-start | bytes 2129920 | tf_op jit(solution)/shard_map/all_gather | solution.py:164
  112.1 6.1 %copy-start.13 = (s32[256,64]{0,1:T(8,128)S(1)}, s32[256,64]{0,1:T(8,128)}, u32[]{:S(2)}) copy-start(s32[256,64]{0,1:T(8,128)} %param.37) | copy-start | bytes 196612
  116.4 127.8 %all-gather.11.cloned.1.call-start = ((), (), s32[]{:S(2)}) async-start(), calls=%async_computation.2 | async-start | bytes 2129920 | tf_op jit(solution)/shard_map/all_gather | solution.py:164
  116.4 301.1 %collective-permute-start.4 = (bf16[704,1408]{1,0:T(8,128)(2,1)}, bf16[704,1408]{1,0:T(8,128)(2,1)}, u32[]{:S(2)}, u32[]{:S(2)}) collective-permute-start(bf16[704,1408]{1,0:T(8,128)(2,1)} %param.43), channel_id=1, source_target_pairs={{0,64},{64,0},{1,65},{65,1},{2,66},{66,2},{3,67},{67,3},{4,68},{68... | collective-permute-start | bytes 5947400 | tf_op jit(solution)/shard_map/ppermute | solution.py:45
  119.3 202.5 %all-gather.13.cloned.1.call-start = ((), (), s32[]{:S(2)}) async-start(), calls=%async_computation.3 | async-start | bytes 2129920 | tf_op jit(solution)/shard_map/all_gather | solution.py:164
  122.6 253.6 %all-gather.15.cloned.1.call-start = ((), (), s32[]{:S(2)}) async-start(), calls=%async_computation.4 | async-start | bytes 2129920 | tf_op jit(solution)/shard_map/all_gather | solution.py:164
  129.7 263.2 %copy-start.5 = (bf16[256,8,88]{2,1,0:T(8,128)(2,1)}, bf16[256,8,88]{2,1,0:T(8,128)(2,1)S(1)}, u32[]{:S(2)}) copy-start(bf16[256,8,88]{2,1,0:T(8,128)(2,1)S(1)} %multiply_convert_fusion.2) | copy-start | bytes 1081348
  251.1 10.0 %copy-start.7 = (pred[192,4096]{1,0:T(8,128)(4,1)S(1)}, pred[192,4096]{1,0:T(8,128)(4,1)}, u32[]{:S(2)}) copy-start(pred[192,4096]{1,0:T(8,128)(4,1)} %compare_and_fusion.1) | copy-start | bytes 2359300
  284.1 16.5 %copy-start.6 = (pred[256,4096]{1,0:T(8,128)(4,1)S(1)}, pred[256,4096]{1,0:T(8,128)(4,1)}, u32[]{:S(2)}) copy-start(pred[256,4096]{1,0:T(8,128)(4,1)} %compare_and_fusion) | copy-start | bytes 3145732
  284.1 16.5 %copy-start.9 = (bf16[4096,1,88]{0,2,1:T(8,128)(2,1)S(1)}, bf16[4096,1,88]{0,2,1:T(8,128)(2,1)}, u32[]{:S(2)}) copy-start(bf16[4096,1,88]{0,2,1:T(8,128)(2,1)} %copy.197) | copy-start | bytes 2162692
  393.0 3.9 copy-start.10
  393.0 3.9 copy-start.14
  396.9 3.7 copy-start.16
  396.9 4.1 slice-start
  396.9 4.1 copy-start.11
  401.0 5.7 %copy-start.8 = (bf16[4096,1,88]{0,2,1:T(8,128)(2,1)S(1)}, bf16[4096,1,88]{0,2,1:T(8,128)(2,1)}, u32[]{:S(2)}) copy-start(bf16[4096,1,88]{0,2,1:T(8,128)(2,1)} %copy.201) | copy-start | bytes 2162692
  415.2 0.7 copy-start.12
  415.9 2.9 collective-permute-start.3
  418.8 6.0 %copy-start.1 = (bf16[1408,704]{0,1:T(8,128)(2,1)S(1)}, bf16[1408,704]{0,1:T(8,128)(2,1)}, u32[]{:S(2)}) copy-start(bf16[1408,704]{0,1:T(8,128)(2,1)} %param.41) | copy-start | bytes 5947396
Sparse Core Ops, SparseCore 0:
  116.5 61.5 all-gather.8
  181.0 63.1 all-gather.10
  247.1 63.1 all-gather.12
  313.0 63.1 all-gather.14
